TPU v7x, 128 devices: a whole 4x4x4 slice. The times are simulated.
128 devices in a mesh: layer: 16 (over y, x), prow: 4 (over z), pcol: 2 (over core).
Axes of the slice: x: 4, y: 4, z: 4, core: 2. Of those that a mesh axis runs over, the one named last changes fastest.
Arguments:
- front: bfloat16 [16, 2048, 32768], P('layer', 'prow', 'pcol'), may hold values from -6 to 6
- pivots: bfloat16 [16, 2, 256, 32768], P('layer', None, 'prow', 'pcol'), may hold values from -0.8984375 to 0.8984375
- inverses: bfloat16 [16, 2, 256, 256], P('layer'), may hold values from -0.1875 to 0.1875
- slab_pattern: int32 [16, 8, 128], P('layer', 'prow', 'pcol'), may hold values 0 or 1
- pivot_pattern: int32 [16, 2, 128], P('layer', None, 'pcol'), may hold values from 0 to 1, as said below
Outputs:
- ancestor: float32 [4, 16, 32, 32768], P('prow', 'layer', None, 'pcol')
- lower: bfloat16 [16, 2048, 512], P('layer', 'prow')
- upper: bfloat16 [16, 256, 32768], P('layer', 'prow', 'pcol')
Inputs may be any that keep to these rules, and one draw needn't show every extreme that they name: `pivot_pattern`: each entry says whether that block of the pivot rows is structurally nonzero. `slab_pattern`: each entry says whether that block of the front rows is structurally nonzero.
All inputs are finite; a program needn't handle non-finite values.
Results may differ from a plain program's by a relative error of at most 0.014.
Values may be sent and summed in bfloat16 or wider, within the bound.
No kernel may reach another device: no remote copies, remote signals or barrier semaphores. Data moves between devices by JAX's collectives and lax.ppermute only.
A program may use at most 192 MiB of HBM per device.

v0:
```python
import jax
import jax.numpy as jnp
from jax import lax
from jax.sharding import PartitionSpec as P


def spread(value, axis, root):
    mine = lax.axis_index(axis) == root
    return lax.psum(jnp.where(mine, value, jnp.zeros_like(value)), axis)


def on_device(front, pivots, inverses, slab_pattern, pivot_pattern):
    block_size = inverses.shape[-1]
    panel_width = 2 * block_size
    row_count = front.shape[1]
    col_count = front.shape[2]
    own_rows = pivots.shape[2]
    masked = (
        front[0].reshape(row_count // block_size, block_size, col_count // block_size, block_size)
        * slab_pattern[0].astype(jnp.bfloat16)[:, None, :, None]
    ).reshape(row_count, col_count)
    pivot_masked = (
        pivots[0].reshape(2, own_rows, col_count // block_size, block_size)
        * pivot_pattern[0].astype(jnp.bfloat16)[:, None, :, None]
    ).reshape(2, own_rows, col_count)
    first_inverse = inverses[0, 0]
    second_inverse = inverses[0, 1]
    row_offset = lax.axis_index("prow") * own_rows
    gathered = lax.all_gather(pivot_masked, "prow", axis=1, tiled=True)
    panel_cols = spread(
        jnp.concatenate(
            [masked[:, :panel_width], gathered[0][:, :panel_width], gathered[1][:, :panel_width]], 0
        ),
        "pcol",
        0,
    )
    front_cols = panel_cols[:row_count]
    pivot_cols = panel_cols[row_count : row_count + block_size]
    second_cols = panel_cols[row_count + block_size :]
    lower_pivot = jnp.dot(
        second_cols[:, :block_size], first_inverse, preferred_element_type=jnp.float32
    ).astype(jnp.bfloat16)
    upper_first = gathered[0]
    upper_second = (
        gathered[1].astype(jnp.float32)
        - jnp.dot(lower_pivot, upper_first, preferred_element_type=jnp.float32)
    ).astype(jnp.bfloat16)
    upper_own = lax.dynamic_slice_in_dim(upper_second, row_offset, own_rows, 0)
    lower_first = jnp.dot(
        front_cols[:, :block_size], first_inverse, preferred_element_type=jnp.float32
    ).astype(jnp.bfloat16)
    carried = (
        front_cols[:, block_size:].astype(jnp.float32)
        - jnp.dot(
            lower_first, pivot_cols[:, block_size:panel_width], preferred_element_type=jnp.float32
        )
    ).astype(jnp.bfloat16)
    lower_second = jnp.dot(carried, second_inverse, preferred_element_type=jnp.float32).astype(
        jnp.bfloat16
    )
    lower_panel = jnp.concatenate([lower_first, lower_second], 1)
    stacked = jnp.concatenate([upper_first, upper_second], 0)
    col_index = lax.axis_index("pcol") * col_count + jnp.arange(col_count, dtype=jnp.int32)
    retained = col_index >= panel_width
    schur_rows = masked.astype(jnp.float32) - jnp.dot(
        lower_panel, stacked, preferred_element_type=jnp.float32
    )
    schur_rows = jnp.where(retained[None, :], schur_rows, jnp.zeros_like(schur_rows))
    summed = lax.psum_scatter(
        schur_rows.astype(jnp.bfloat16), "layer", scatter_dimension=0, tiled=True
    ).astype(jnp.float32)
    ancestor = summed.reshape(1, 1, summed.shape[0], col_count)
    return (ancestor, lower_panel[None], upper_own[None])


def solution(mesh):
    placed = (
        P("layer", "prow", "pcol"),
        P("layer", None, "prow", "pcol"),
        P("layer", None, None, None),
        P("layer", "prow", "pcol"),
        P("layer", None, "pcol"),
    )
    return jax.shard_map(
        on_device,
        mesh=mesh,
        in_specs=placed,
        out_specs=(
            P("prow", "layer", None, "pcol"),
            P("layer", "prow", None),
            P("layer", "prow", "pcol"),
        ),
        check_vma=False,
    )
```

profile of v0, /device:TPU:1, one launch (start us, length us, event | category | flops | bytes accessed | tf_op | source)
XLA Modules:
  0.0 362.8 jit_solution(13036660158709411677)
XLA Ops:
  7.2 0.0 all-gather.2.cloned.1.call-start
  7.2 0.7 convert_bitcast_fusion
  7.9 0.1 broadcast_bitcast_fusion
  8.0 0.1 copy.10
  8.1 4.8 %bitcast_multiply_fusion.1 = bf16[2,64,16384]{2,1,0:T(8,128)(2,1)} fusion(bf16[1,2,64,16384]{3,2,1,0:T(8,128)(2,1)} %param.6, bf16[2,16384]{1,0:T(2,128)(2,1)S(1)} %bitcast.40), kind=kLoop, calls=%fused_computation.9 | loop fusion | flops 2097152 | bytes 8454144 | tf_op jit(solution)/shard_map/mul | solution.py:23
  12.8 0.0 all-gather.2.cloned.1.call-update
  12.9 0.0 all-reduce.2.cloned.1.call-start
  12.9 0.7 convert_bitcast_fusion.1
  13.6 2.7 mul.31
  16.3 10.4 %copy.9 = bf16[64,8,64,256]{3,1,2,0:T(8,128)(2,1)S(1)} copy(bf16[64,8,64,256]{3,2,1,0:T(8,128)(2,1)S(1)} %bitcast.39) | data formatting | bytes 33554432
  26.8 9.7 %bitcast_multiply_fusion = bf16[512,16384]{1,0:T(8,128)(2,1)S(1)} fusion(bf16[512,16384]{1,0:T(8,128)(2,1)S(1)} %bitcast.38, bf16[1,512,16384]{2,1,0:T(8,128)(2,1)} %param.5), kind=kLoop, calls=%fused_computation.6 | loop fusion | flops 8388608 | bytes 50331648 | tf_op jit(solution)/shard_map/mul | solution.py:19
  36.5 0.0 copy-start
  36.5 5.9 %copy-done = bf16[512,16384]{1,0:T(8,128)(2,1)} copy-done((bf16[512,16384]{1,0:T(8,128)(2,1)}, bf16[512,16384]{1,0:T(8,128)(2,1)S(1)}, u32[]{:S(2)}) %copy-start) | copy-done | bytes 16777240
  42.5 0.0 copy-start.2
  42.5 127.9 %all-gather.2.cloned.1.call-done = bf16[2,256,16384]{2,1,0:T(8,128)(2,1)} async-done(((bf16[2,64,16384]{2,1,0:T(8,128)(2,1)}), bf16[2,256,16384]{2,1,0:T(8,128)(2,1)}) %all-gather.2.cloned.1.call-update) | async-done | bytes 16777232 | tf_op jit(solution)/shard_map/all_gather | solution.py:29
  170.4 6.7 %slice_bitcast_fusion.1 = (bf16[256,16384]{1,0:T(8,128)(2,1)S(1)}, bf16[256,16384]{1,0:T(8,128)(2,1)S(1)}) fusion(bf16[2,256,16384]{2,1,0:T(8,128)(2,1)} %all-gather.2.cloned.1.call-done), kind=kLoop, calls=%fused_computation.8 | loop fusion | bytes 33554432 | tf_op jit(solution)/shard_map/squeeze | solution.py:32
  177.1 0.0 copy-start.1
  177.2 3.2 copy-done.1
  180.4 1.2 maximum_select_fusion
  181.6 0.0 all-reduce.2.cloned.1.call-update
  181.6 0.0 reduce-scatter.2.cloned.1.call-start
  181.7 26.6 %all-reduce.2.cloned.1.call-done = bf16[1024,512]{1,0:T(8,128)(2,1)} async-done(((bf16[1024,512]{1,0:T(8,128)(2,1)}), bf16[1024,512]{1,0:T(8,128)(2,1)}) %all-reduce.2.cloned.1.call-update) | async-done | bytes 1048592 | tf_op jit(solution)/shard_map/psum | solution.py:9
  208.3 0.0 copy-done.2
  208.3 9.3 %fusion = bf16[256,16384]{1,0:T(8,128)(2,1)} fusion(bf16[1024,512]{1,0:T(8,128)(2,1)} %all-reduce.2.cloned.1.call-done, bf16[1,2,256,256]{3,2,1,0:T(8,128)(2,1)S(1)} %copy-done.2, bf16[2,256,16384]{2,1,0:T(8,128)(2,1)} %all-gather.2.cloned.1.call-done), kind=kOutput, calls=%fused_computation.2 | convolution fusion | flops 2193686528 | bytes 25427968 | tf_op jit(solution)/shard_map/dot_general | solution.py:46
  217.6 1.2 convolution_convert_fusion.1
  218.8 1.5 convolution_convert_fusion
  220.3 22.0 %select_convert_fusion = bf16[512,16384]{1,0:T(8,128)(2,1)} fusion(bf16[512,16384]{1,0:T(8,128)(2,1)} %copy-done, bf16[256,16384]{1,0:T(8,128)(2,1)} %fusion, bf16[256,16384]{1,0:T(8,128)(2,1)} %copy-done.1, pred[16384]{0:T(1024)(128)(4,1)S(1)} %add_compare_fusion, bf16[512,256]{0,1:T(8,128)(2,1)S(1)} %convolution_convert_fusion, ...), kind=kOutput, calls=%fused_computation | convolution fusion | flops 8658092032 | bytes 50872320 | tf_op jit(solution)/shard_map/dot_general | solution.py:65
  242.2 0.0 reduce-scatter.2.cloned.1.call-update
  242.3 1.0 copy.8
  243.3 3.0 dynamic-slice_bitcast_fusion
  246.4 107.2 %reduce-scatter.2.cloned.1.call-done = bf16[32,16384]{1,0:T(8,128)(2,1)} async-done(((bf16[512,16384]{1,0:T(8,128)(2,1)}), bf16[32,16384]{1,0:T(8,128)(2,1)}) %reduce-scatter.2.cloned.1.call-update) | async-done | bytes 1048592 | tf_op jit(solution)/shard_map/reduce_scatter | solution.py:69
  353.6 2.7 bitcast_convert_fusion
  (5 shorter events, 0.1 us)
Async XLA Ops:
  7.2 163.2 %all-gather.2.cloned.1.call-start = ((), (), s32[]{:S(2)}) async-start(), calls=%async_computation.1 | async-start | bytes 20971520 | tf_op jit(solution)/shard_map/all_gather | solution.py:29
  12.9 195.4 %all-reduce.2.cloned.1.call-start = ((), (), s32[]{:S(2)}) async-start(), calls=%async_computation.2 | async-start | bytes 2097152 | tf_op jit(solution)/shard_map/psum | solution.py:9
  36.5 6.0 %copy-start = (bf16[512,16384]{1,0:T(8,128)(2,1)}, bf16[512,16384]{1,0:T(8,128)(2,1)S(1)}, u32[]{:S(2)}) copy-start(bf16[512,16384]{1,0:T(8,128)(2,1)S(1)} %bitcast_multiply_fusion) | copy-start | bytes 50331652
  42.5 165.8 %copy-start.2 = (bf16[1,2,256,256]{3,2,1,0:T(8,128)(2,1)S(1)}, bf16[1,2,256,256]{3,2,1,0:T(8,128)(2,1)}, u32[]{:S(2)}) copy-start(bf16[1,2,256,256]{3,2,1,0:T(8,128)(2,1)} %param.7) | copy-start | bytes 786436
  177.1 3.2 copy-start.1
  181.6 172.0 %reduce-scatter.2.cloned.1.call-start = ((), (), s32[]{:S(2)}) async-start(), calls=%async_computation.3 | async-start | bytes 17825792 | tf_op jit(solution)/shard_map/reduce_scatter | solution.py:69
Sparse Core Ops, SparseCore 0:
  13.0 157.3 all-gather.1
  181.7 26.5 all-reduce.1
  242.4 111.1 reduce-scatter.1
where the time goes:
time: 363 us
  waiting for transfers between devices  262 us (72%)
  matrix products  33.9 us (9%)
  local copies, waits for them, and re-layouts  33.3 us (9%)
  other arithmetic  19.8 us (5%)
  between operations  13.9 us (4%)
    all_gather x1, waiting for transfers between devices, on_device(): gathered = lax.all_gather(pivot_masked, 'prow', axis=1, tiled=True)  128 us
    reduce_scatter x1, waiting for transfers between devices, on_device(): lax.psum_scatter(schur_rows.astype(jnp.bfloat16), 'layer', scatter_dimens...  107 us
    psum x1, waiting for transfers between devices, spread(): return lax.psum(jnp.where(mine, value, jnp.zeros_like(value)), axis)  26.6 us
    dot_general x1, matrix products, on_device(): jnp.dot(lower_panel, stacked, preferred_element_type=jnp.float32)  22 us
    unnamed x10, local copies, waits for them, and re-layouts  20.7 us
    mul x1, other arithmetic, on_device(): front[0]  9.72 us
    dot_general x1, matrix products, on_device(): jnp.dot(lower_pivot, upper_first, preferred_element_type=jnp.float32)  9.25 us
  transfers between devices with their start and end apart: 3, of which 3 were waited for; matrix products, arithmetic and copies ran while one was open for 8% of the time, Pallas kernels for 0%

commit v1 on v0

--- a/solution.py
+++ b/solution.py
@@ -6,7 +6,7 @@
 
 def spread(value, axis, root):
     mine = lax.axis_index(axis) == root
-    return lax.psum(jnp.where(mine, value, jnp.zeros_like(value)), axis)
+    return jnp.sum(lax.all_gather(jnp.where(mine, value, jnp.zeros_like(value)), axis), axis=0)
 
 
 def on_device(front, pivots, inverses, slab_pattern, pivot_pattern):

time: 363 us -> 352 us (0.970)
  waiting for transfers between devices: 262 us -> 244 us
  other arithmetic: 19.8 us -> 26 us
    psum x1 -> x0, waiting for transfers between devices: 26.6 us -> none  [spread(): return lax.psum(jnp.where(mine, value, jnp.zeros_like(value)), axis)]
    all_gather x0 -> x1, waiting for transfers between devices: none -> 14.8 us  [spread(): lax.all_gather(jnp.where(mine, value, jnp.zeros_like(value)), axis)]
    all_gather x1, waiting for transfers between devices: 128 us -> 122 us  [on_device(): gathered = lax.all_gather(pivot_masked, 'prow', axis=1, tiled=True)]
    mul x1, other arithmetic: 9.72 us -> 14 us  [on_device(): front[0]]
    unnamed x10 -> x12, local copies, waits for them, and re-layouts: 20.7 us -> 22.5 us
  transfers between devices with their start and end apart: 3 -> 3, of which waited for: 3 -> 3; matrix products, arithmetic and copies ran while one was open for 8% -> 9% of each run, Pallas kernels for 0% -> 0%
where the time goes in v1:
time: 352 us; the launch traced here: 351 us
  waiting for transfers between devices  244 us (69%)
  local copies, waits for them, and re-layouts  35.1 us (10%)
  matrix products  32.1 us (9%)
  other arithmetic  26 us (7%)
  between operations  13.9 us (4%)
    all_gather x1, waiting for transfers between devices, on_device(): gathered = lax.all_gather(pivot_masked, 'prow', axis=1, tiled=True)  122 us
    reduce_scatter x1, waiting for transfers between devices, on_device(): lax.psum_scatter(schur_rows.astype(jnp.bfloat16), 'layer', scatter_dimens...  107 us
    unnamed x12, local copies, waits for them, and re-layouts  22.5 us
    dot_general x1, matrix products, on_device(): jnp.dot(lower_panel, stacked, preferred_element_type=jnp.float32)  21.9 us
    all_gather x1, waiting for transfers between devices, spread(): lax.all_gather(jnp.where(mine, value, jnp.zeros_like(value)), axis)  14.8 us
    mul x1, other arithmetic, on_device(): front[0]  14 us
    dot_general x1, matrix products, on_device(): jnp.dot(lower_pivot, upper_first, preferred_element_type=jnp.float32)  9.43 us
  transfers between devices with their start and end apart: 3, of which 3 were waited for; matrix products, arithmetic and copies ran while one was open for 9% of the time, Pallas kernels for 0%

profile of v1, /device:TPU:1, one launch (start us, length us, event | category | flops | bytes accessed | tf_op | source)
XLA Modules:
  0.0 351.5 jit_solution(7392531892863243892)
XLA Ops:
  7.2 0.0 copy-start.3
  7.2 0.0 all-gather.3.cloned.1.call-start
  7.2 0.7 convert_bitcast_fusion
  7.9 0.1 broadcast_bitcast_fusion
  8.0 0.1 copy.11
  8.1 4.8 %bitcast_multiply_fusion.1 = bf16[2,64,16384]{2,1,0:T(8,128)(2,1)} fusion(bf16[1,2,64,16384]{3,2,1,0:T(8,128)(2,1)} %param.6, bf16[2,16384]{1,0:T(2,128)(2,1)S(1)} %bitcast.46), kind=kLoop, calls=%fused_computation.9 | loop fusion | flops 2097152 | bytes 8454144 | tf_op jit(solution)/shard_map/mul | solution.py:23
  12.9 0.0 all-gather.3.cloned.1.call-update
  12.9 0.0 all-gather.5.cloned.1.call-start
  12.9 0.0 copy-done.3
  13.0 2.7 mul.31
  15.7 12.4 %copy.10 = bf16[64,8,64,256]{3,1,2,0:T(8,128)(2,1)} copy(bf16[64,8,64,256]{3,2,1,0:T(8,128)(2,1)S(1)} %bitcast.45) | data formatting | bytes 33554432
  28.2 14.0 %bitcast_multiply_fusion = bf16[512,16384]{1,0:T(8,128)(2,1)S(1)} fusion(bf16[512,16384]{1,0:T(8,128)(2,1)} %bitcast.44, bf16[1,512,16384]{2,1,0:T(8,128)(2,1)} %param.5), kind=kLoop, calls=%fused_computation.6 | loop fusion | flops 8388608 | bytes 50331648 | tf_op jit(solution)/shard_map/mul | solution.py:19
  42.2 0.0 copy-start
  42.2 5.7 %copy-done = bf16[512,16384]{1,0:T(8,128)(2,1)} copy-done((bf16[512,16384]{1,0:T(8,128)(2,1)}, bf16[512,16384]{1,0:T(8,128)(2,1)S(1)}, u32[]{:S(2)}) %copy-start) | copy-done | bytes 16777240
  48.0 0.0 copy-start.2
  48.0 122.4 %all-gather.3.cloned.1.call-done = bf16[2,256,16384]{2,1,0:T(8,128)(2,1)} async-done(((bf16[2,64,16384]{2,1,0:T(8,128)(2,1)}), bf16[2,256,16384]{2,1,0:T(8,128)(2,1)}) %all-gather.3.cloned.1.call-update) | async-done | bytes 16777232 | tf_op jit(solution)/shard_map/all_gather | solution.py:29
  170.4 6.7 %slice_bitcast_fusion.1 = (bf16[256,16384]{1,0:T(8,128)(2,1)S(1)}, bf16[256,16384]{1,0:T(8,128)(2,1)S(1)}) fusion(bf16[2,256,16384]{2,1,0:T(8,128)(2,1)} %all-gather.3.cloned.1.call-done), kind=kLoop, calls=%fused_computation.8 | loop fusion | bytes 33554432 | tf_op jit(solution)/shard_map/squeeze | solution.py:32
  177.2 0.0 copy-start.1
  177.2 3.2 copy-done.1
  180.4 1.2 maximum_select_fusion
  181.6 0.0 all-gather.5.cloned.1.call-update
  181.6 0.0 reduce-scatter.2.cloned.1.call-start
  181.7 14.8 %all-gather.5.cloned.1.call-done = bf16[2,1024,512]{2,1,0:T(8,128)(2,1)} async-done(((bf16[1,1024,512]{2,1,0:T(8,128)(2,1)}), bf16[2,1024,512]{2,1,0:T(8,128)(2,1)}) %all-gather.5.cloned.1.call-update) | async-done | bytes 2097168 | tf_op jit(solution)/shard_map/all_gather | solution.py:9
  196.5 2.6 reduce_sum.12
  199.1 0.0 copy-done.2
  199.1 0.3 convolution_convert_fusion.1
  199.4 0.5 convolution_convert_fusion
  199.8 9.4 %fusion = bf16[256,16384]{1,0:T(8,128)(2,1)} fusion(bf16[1024,512]{1,0:T(8,128)(2,1)S(1)} %reduce_sum.12, bf16[1,2,256,256]{3,2,1,0:T(8,128)(2,1)S(1)} %copy-done.2, bf16[2,256,16384]{2,1,0:T(8,128)(2,1)} %all-gather.3.cloned.1.call-done), kind=kOutput, calls=%fused_computation.2 | convolution fusion | flops 2193686528 | bytes 25427968 | tf_op jit(solution)/shard_map/dot_general | solution.py:46
  209.3 21.9 %select_convert_fusion = bf16[512,16384]{1,0:T(8,128)(2,1)} fusion(bf16[512,16384]{1,0:T(8,128)(2,1)} %copy-done, bf16[256,16384]{1,0:T(8,128)(2,1)} %fusion, bf16[256,16384]{1,0:T(8,128)(2,1)} %copy-done.1, pred[16384]{0:T(1024)(128)(4,1)S(1)} %add_compare_fusion, bf16[512,256]{0,1:T(8,128)(2,1)S(1)} %convolution_convert_fusion, ...), kind=kOutput, calls=%fused_computation | convolution fusion | flops 8658092032 | bytes 50872320 | tf_op jit(solution)/shard_map/dot_general | solution.py:65
  231.2 0.0 reduce-scatter.2.cloned.1.call-update
  231.2 1.0 copy.9
  232.2 3.0 dynamic-slice_bitcast_fusion
  235.3 107.0 %reduce-scatter.2.cloned.1.call-done = bf16[32,16384]{1,0:T(8,128)(2,1)} async-done(((bf16[512,16384]{1,0:T(8,128)(2,1)}), bf16[32,16384]{1,0:T(8,128)(2,1)}) %reduce-scatter.2.cloned.1.call-update) | async-done | bytes 1048592 | tf_op jit(solution)/shard_map/reduce_scatter | solution.py:69
  342.3 2.7 bitcast_convert_fusion
  (5 shorter events, 0.1 us)
Async XLA Ops:
  7.2 5.8 %copy-start.3 = (s32[1,2,64]{2,1,0:T(2,128)S(1)}, s32[1,2,64]{2,1,0:T(2,128)}, u32[]{:S(2)}) copy-start(s32[1,2,64]{2,1,0:T(2,128)} %param.8) | copy-start | bytes 1540
  7.2 163.2 %all-gather.3.cloned.1.call-start = ((), (), s32[]{:S(2)}) async-start(), calls=%async_computation.1 | async-start | bytes 20971520 | tf_op jit(solution)/shard_map/all_gather | solution.py:29
  12.9 183.6 %all-gather.5.cloned.1.call-start = ((), (), s32[]{:S(2)}) async-start(), calls=%async_computation.2 | async-start | bytes 3145728 | tf_op jit(solution)/shard_map/all_gather | solution.py:9
  42.2 5.7 %copy-start = (bf16[512,16384]{1,0:T(8,128)(2,1)}, bf16[512,16384]{1,0:T(8,128)(2,1)S(1)}, u32[]{:S(2)}) copy-start(bf16[512,16384]{1,0:T(8,128)(2,1)S(1)} %bitcast_multiply_fusion) | copy-start | bytes 50331652
  48.0 151.1 %copy-start.2 = (bf16[1,2,256,256]{3,2,1,0:T(8,128)(2,1)S(1)}, bf16[1,2,256,256]{3,2,1,0:T(8,128)(2,1)}, u32[]{:S(2)}) copy-start(bf16[1,2,256,256]{3,2,1,0:T(8,128)(2,1)} %param.7) | copy-start | bytes 786436
  177.2 3.2 copy-start.1
  181.6 160.6 %reduce-scatter.2.cloned.1.call-start = ((), (), s32[]{:S(2)}) async-start(), calls=%async_computation.3 | async-start | bytes 17825792 | tf_op jit(solution)/shard_map/reduce_scatter | solution.py:69
Sparse Core Ops, SparseCore 0:
  13.0 157.3 all-gather.2
  181.7 14.6 all-gather.4
  231.3 110.9 reduce-scatter.1
